TPU v7x, 512 devices: a whole 4x4x16 slice. The times are simulated.
512 devices in a mesh: pool: 128 (over x, z, core), tp: 4 (over y).
Axes of the slice: x: 4, y: 4, z: 16, core: 2. Of those that a mesh axis runs over, the one named last changes fastest.
Arguments:
- hidden_rows: bfloat16 [16384, 8192], P('pool', 'tp'), may hold values from -6 to 6
- kv_weight: bfloat16 [8192, 1024], P('tp', 'pool'), may hold values from -0.0625 to 0.0625
- queries: bfloat16 [16384, 4096], P('pool', 'tp'), may hold values from -5 to 5
- cache_table: bfloat16 [1024, 128, 1024], P('pool', None, 'tp'), may hold values from -5 to 5
- retrieval: int32 [128, 64], P('pool'), may hold values from 0 to 1023, as said below
- pattern: int32 [128, 2, 64], P('pool'), may hold values 0 or 1
Outputs:
- attended: bfloat16 [16384, 4096], P('pool', 'tp')
- fresh_kv: bfloat16 [16384, 1024], P('pool', 'tp')
Inputs may be any that keep to these rules, and one draw needn't show every extreme that they name: `retrieval`: each request names 64 blocks held by 64 different devices (block b is held by device b // 8); one device, drawn from the seed, holds a block named by every request.
All inputs are finite; a program needn't handle non-finite values. No bound on the sum of `pattern` on one device may be relied on, other than what follows from the above.
Results may differ from a plain program's by a relative error of at most 0.025.
Values may be sent and summed in bfloat16 or wider, within the bound.
No kernel may reach another device: no remote copies, remote signals or barrier semaphores. Data moves between devices by JAX's collectives and lax.ppermute only.
A program may use at most 192 MiB of HBM per device.

v0:
```python
import math
import jax
import jax.numpy as jnp
from jax import lax
from jax.sharding import PartitionSpec as P

HD = 128
QH = 32
KVH = 4
BLK = 128
RBLK = 64


def rows_by_keys(left, right):
    return lax.dot_general(
        left, right, (((1,), (1,)), ((), ())), preferred_element_type=jnp.float32
    )


def body(hidden_rows, kv_weight, queries, cache_table, retrieval, pattern):
    partial_kv = jnp.dot(
        hidden_rows,
        lax.all_gather(kv_weight, "pool", axis=1, tiled=True),
        preferred_element_type=jnp.float32,
    )
    fresh = lax.psum_scatter(partial_kv.astype(jnp.bfloat16), "tp", scatter_dimension=1, tiled=True)
    wanted = retrieval[0]
    npool = lax.axis_size("pool")
    by_token = lax.all_to_all(cache_table, "pool", split_axis=1, concat_axis=0, tiled=True)
    by_token = by_token.reshape(by_token.shape[0], by_token.shape[2])
    wanted_all = lax.all_gather(retrieval, "pool", axis=0, tiled=True)
    reply = jnp.take(by_token, wanted_all, axis=0)
    fetched = lax.all_to_all(reply[:, :, None, :], "pool", split_axis=0, concat_axis=2, tiled=True)[
        0
    ]
    count = hidden_rows.shape[0]
    fetch_count = wanted.shape[0]
    group = QH // KVH
    scale = float(HD) ** (-0.5)
    local_heads = fresh.shape[1] // (2 * HD)
    width = fetched.shape[2]
    per_step = math.gcd(fetch_count, 8)
    steps_count = fetch_count // per_step
    grouped = fetched.reshape(steps_count, per_step * BLK, width)
    pat_steps = jnp.transpose(
        pattern[0].reshape(pattern.shape[1], steps_count, per_step), (1, 0, 2)
    )
    token_of_row = jnp.arange(count * group) // group
    block_of_row = token_of_row // RBLK
    row_blocks = block_of_row[:, None, None] == jnp.arange(pattern.shape[1])[None, :, None]
    near_mask = token_of_row[:, None] >= jnp.arange(count)[None, :]
    q_heads = queries.reshape(count, local_heads, group * HD)
    q_rows = q_heads[:, 0].reshape(count * group, HD)
    near_keys = fresh[:, 0:HD]
    near_vals = fresh[:, HD : 2 * HD]
    near_scores = rows_by_keys(q_rows, near_keys) * scale
    top = jnp.max(jnp.where(near_mask, near_scores, -1e30), axis=1)
    weights = jnp.where(near_mask, jnp.exp(near_scores - top[:, None]), 0.0)
    total = jnp.sum(weights, axis=1)
    numer = jnp.dot(weights.astype(jnp.bfloat16), near_vals, preferred_element_type=jnp.float32)

    def visit(carry, items):
        top_now, total_now, numer_now = carry
        block_rows, pat_now = items
        keys = block_rows[:, 0:HD]
        vals = block_rows[:, HD : 2 * HD]
        scores = rows_by_keys(q_rows, keys) * scale
        row_pat = jnp.any(row_blocks & (pat_now[None] != 0), axis=1)
        mask = jnp.repeat(row_pat, BLK, axis=1)
        top_new = jnp.maximum(top_now, jnp.max(jnp.where(mask, scores, -1e30), axis=1))
        weights_now = jnp.where(mask, jnp.exp(scores - top_new[:, None]), 0.0)
        factor = jnp.exp(top_now - top_new)
        total_new = total_now * factor + jnp.sum(weights_now, axis=1)
        numer_new = numer_now * factor[:, None] + jnp.dot(
            weights_now.astype(jnp.bfloat16), vals, preferred_element_type=jnp.float32
        )
        return ((top_new, total_new, numer_new), None)

    (top, total, numer), unused = lax.scan(visit, (top, total, numer), (grouped, pat_steps))
    results = (numer / total[:, None]).reshape(count, group * HD)
    attended = results.astype(jnp.bfloat16)
    return (attended, fresh)


def solution(mesh):
    placed = (
        P("pool", "tp"),
        P("tp", "pool"),
        P("pool", "tp"),
        P("pool", None, "tp"),
        P("pool", None),
        P("pool", None, None),
    )
    return jax.shard_map(
        body,
        mesh=mesh,
        in_specs=placed,
        out_specs=(P("pool", "tp"), P("pool", "tp")),
        check_vma=False,
    )
```

profile of v0, /device:TPU:4, one launch (start us, length us, event | category | flops | bytes accessed | tf_op | source)
XLA Modules:
  0.0 440.1 jit_solution(318980175920545042)
XLA Ops:
  7.2 2.2 copy.24
  9.4 19.7 %all-to-all-start = ((bf16[8,128,256]{2,0,1:T(8,128)(2,1)}), bf16[8,128,256]{2,0,1:T(8,128)(2,1)S(1)}, u32[]{:S(2)}, u32[]{:S(2)}) async-start(bf16[8,128,256]{2,0,1:T(8,128)(2,1)} %copy.24), calls=%async_computation.1 | async-start | bytes 1048576 | tf_op jit(solution)/shard_map/all_to_all | solution.py:29
  29.1 92.0 %all-gather = s32[128,1,64]{2,1,0:T(1,128)S(1)} all-gather(s32[1,1,64]{2,1,0:T(1,128)} %bitcast.77), channel_id=1, replica_groups=mesh['pool'=128,'tp'=4] {'pool'}, dimensions={0}, use_global_device_ids=true | all-gather | bytes 33024 | tf_op jit(solution)/shard_map/all_gather | solution.py:31
  121.2 33.1 %gather_fusion = bf16[8192,256]{1,0:T(8,128)(2,1)} fusion(bf16[1024,256]{1,0:T(8,128)(2,1)S(1)} %bitcast.70, s32[8192]{0:T(1024)S(1)} %broadcast_clamp_fusion), kind=kCustom, calls=%fused_computation | custom fusion | bytes 8421376 | tf_op jit(solution)/shard_map/jit(_take)/gather | solution.py:32
  154.4 5.2 %broadcast_select_fusion = bf16[128,64,1,256]{3,1,2,0:T(8,128)(2,1)} fusion(bf16[128,64,1,256]{3,1,2,0:T(8,128)(2,1)} %bitcast.71, pred[128,64]{1,0:T(8,128)(4,1)S(1)} %compare_and_fusion), kind=kLoop, calls=%fused_computation.20 | loop fusion | flops 2097152 | bytes 8396800 | tf_op jit(solution)/shard_map/jit(_take)/select_n | solution.py:32
  159.6 14.0 %all-to-all-start.1 = ((bf16[128,64,1,256]{3,1,2,0:T(8,128)(2,1)}), bf16[128,64,1,256]{3,1,2,0:T(8,128)(2,1)}, u32[]{:S(2)}, u32[]{:S(2)}) async-start(bf16[128,64,1,256]{3,1,2,0:T(8,128)(2,1)} %broadcast_select_fusion), calls=%async_computation.2 | async-start | bytes 8388608 | tf_op jit(solution)/shard_map/all_to_all | solution.py:33
  173.7 0.7 all-gather.3.cloned.1.call-update
  174.4 0.2 reduce-scatter.2.cloned.1.call-start
  174.6 183.9 %all-gather.3.cloned.1.call-done = bf16[2048,1024]{0,1:T(8,128)(2,1)} async-done(((bf16[2048,8]{0,1:T(8,128)(2,1)}), bf16[2048,1024]{0,1:T(8,128)(2,1)}) %all-gather.3.cloned.1.call-update) | async-done | bytes 4194320 | tf_op jit(solution)/shard_map/all_gather | solution.py:23
  358.5 4.4 %convolution_convert_fusion = bf16[128,1024]{1,0:T(8,128)(2,1)} fusion(bf16[128,2048]{1,0:T(8,128)(2,1)S(1)} %copy-done, bf16[2048,1024]{0,1:T(8,128)(2,1)} %all-gather.3.cloned.1.call-done), kind=kOutput, calls=%fused_computation.23 | convolution fusion | flops 537001984 | bytes 4980736 | tf_op jit(solution)/shard_map/dot_general | solution.py:21
  363.1 29.0 %reduce-scatter.2.cloned.1.call-done = bf16[128,256]{1,0:T(8,128)(2,1)} async-done(((bf16[128,1024]{1,0:T(8,128)(2,1)}), bf16[128,256]{1,0:T(8,128)(2,1)}) %reduce-scatter.2.cloned.1.call-update) | async-done | bytes 65552 | tf_op jit(solution)/shard_map/reduce_scatter | solution.py:26
  392.1 1.0 select_reduce_fusion
  393.3 1.0 fusion.12
  394.3 6.5 %copy.26 = bf16[128,64,1,256]{3,0,1,2:T(8,128)(2,1)} copy(bf16[128,64,1,256]{3,1,2,0:T(8,128)(2,1)} %all-to-all-done.1) | data formatting | bytes 8388608 | tf_op jit(solution)/shard_map/all_to_all | solution.py:33
  400.8 31.4 %while.15 = (s32[]{:T(128)}, f32[1024]{0:T(1024)S(1)}, f32[1024]{0:T(1024)S(1)}, f32[1024,128]{1,0:T(8,128)S(1)}, s32[8,2,8]{2,0,1:T(8,128)S(1)}, /*index=5*/bf1...) while((s32[]{:T(128)}, f32[1024]{0:T(1024)S(1)}, ...), condition=%wide.region_7.8_spmd.clone, body=%wide.region_3.7_spmd.clone.sunk | while | flops 545550336 | bytes 15561037 | solution.py:79
  400.9 1.1 dynamic-slice_bitcast_fusion.2
  402.0 0.7 fusion.38
  402.8 0.9 fusion.39
  403.7 1.0 convolution_add_fusion.2
  404.9 1.1 dynamic-slice_bitcast_fusion.2
  405.9 0.7 fusion.38
  406.7 0.9 fusion.39
  407.7 1.0 convolution_add_fusion.2
  408.8 1.1 dynamic-slice_bitcast_fusion.2
  409.9 0.7 fusion.38
  410.6 0.9 fusion.39
  411.6 1.0 convolution_add_fusion.2
  412.7 1.1 dynamic-slice_bitcast_fusion.2
  413.8 0.7 fusion.38
  414.6 0.9 fusion.39
  415.5 1.0 convolution_add_fusion.2
  416.7 1.1 dynamic-slice_bitcast_fusion.2
  417.7 0.7 fusion.38
  418.5 0.9 fusion.39
  419.5 1.0 convolution_add_fusion.2
  420.6 1.1 dynamic-slice_bitcast_fusion.2
  421.7 0.7 fusion.38
  422.4 0.9 fusion.39
  423.4 1.0 convolution_add_fusion.2
  424.5 1.1 dynamic-slice_bitcast_fusion.2
  425.6 0.7 fusion.38
  426.4 0.9 fusion.39
  427.3 1.0 convolution_add_fusion.2
  428.5 1.1 dynamic-slice_bitcast_fusion.2
  429.5 0.7 fusion.38
  430.3 0.9 fusion.39
  431.3 1.0 convolution_add_fusion.2
  432.5 0.8 convert_element_type.18
  (76 shorter events, 1.7 us)
Async XLA Ops:
  7.2 351.3 %copy-start = (bf16[128,2048]{1,0:T(8,128)(2,1)S(1)}, bf16[128,2048]{1,0:T(8,128)(2,1)}, u32[]{:S(2)}) copy-start(bf16[128,2048]{1,0:T(8,128)(2,1)} %param.8) | copy-start | bytes 1572868
  9.4 111.9 %all-to-all-start = ((bf16[8,128,256]{2,0,1:T(8,128)(2,1)}), bf16[8,128,256]{2,0,1:T(8,128)(2,1)S(1)}, u32[]{:S(2)}, u32[]{:S(2)}) async-start(bf16[8,128,256]{2,0,1:T(8,128)(2,1)} %copy.24), calls=%async_computation.1 | async-start | bytes 1048576 | tf_op jit(solution)/shard_map/all_to_all | solution.py:29
  159.6 234.7 %all-to-all-start.1 = ((bf16[128,64,1,256]{3,1,2,0:T(8,128)(2,1)}), bf16[128,64,1,256]{3,1,2,0:T(8,128)(2,1)}, u32[]{:S(2)}, u32[]{:S(2)}) async-start(bf16[128,64,1,256]{3,1,2,0:T(8,128)(2,1)} %broadcast_select_fusion), calls=%async_computation.2 | async-start | bytes 8388608 | tf_op jit(solution)/shard_map/all_to_all | solution.py:33
  173.6 189.3 %copy-start.2 = (s32[1,2,64]{2,1,0:T(2,128)S(1)}, s32[1,2,64]{2,1,0:T(2,128)}, u32[]{:S(2)}) copy-start(s32[1,2,64]{2,1,0:T(2,128)} %param.13) | copy-start | bytes 1540
  173.6 189.4 %copy-start.1 = (bf16[128,1024]{1,0:T(8,128)(2,1)S(1)}, bf16[128,1024]{1,0:T(8,128)(2,1)}, u32[]{:S(2)}) copy-start(bf16[128,1024]{1,0:T(8,128)(2,1)} %param.10) | copy-start | bytes 786436
  173.6 184.8 %all-gather.3.cloned.1.call-start = ((), (), s32[]{:S(2)}) async-start(), calls=%async_computation.3 | async-start | bytes 4227072 | tf_op jit(solution)/shard_map/all_gather | solution.py:23
  174.4 217.8 %reduce-scatter.2.cloned.1.call-start = ((), (), s32[]{:S(2)}) async-start(), calls=%async_computation.4 | async-start | bytes 327680 | tf_op jit(solution)/shard_map/reduce_scatter | solution.py:26
Sparse Core Ops, SparseCore 0:
  177.6 180.8 all-gather.2
  363.0 29.0 reduce-scatter.1
where the time goes:
time: 441 us; the launch traced here: 440 us
  waiting for transfers between devices  214 us (49%)
  blocking collectives  92 us (21%)
  local copies, waits for them, and re-layouts  51.6 us (12%)
  starting transfers between devices  34 us (8%)
  matrix products  20.2 us (5%)
  between operations  14.2 us (3%)
  other arithmetic  14 us (3%)
    all_gather x1, waiting for transfers between devices, body(): lax.all_gather(kv_weight, 'pool', axis=1, tiled=True)  184 us
    all_gather x1, blocking collectives, body(): wanted_all = lax.all_gather(retrieval, 'pool', axis=0, tiled=True)  92 us
    gather x1, local copies, waits for them, and re-layouts, body(): reply = jnp.take(by_token, wanted_all, axis=0)  33.1 us
    reduce_scatter x1, waiting for transfers between devices, body(): lax.psum_scatter(partial_kv.astype(jnp.bfloat16), 'tp', scatter_dimension...  29 us
    all_to_all x1, starting transfers between devices, body(): lax.all_to_all(cache_table, 'pool', split_axis=1, concat_axis=0, tiled=True)  19.7 us
    all_to_all x1, starting transfers between devices, body(): lax.all_to_all(reply[:, :, None, :], 'pool', split_axis=0, concat_axis=2,...  14 us
  transfers between devices with their start and end apart: 4, of which 2 were waited for; matrix products, arithmetic and copies ran while one was open for 2% of the time, Pallas kernels for 0%

commit v1 on v0

--- a/solution.py
+++ b/solution.py
@@ -30,9 +30,13 @@
     by_token = by_token.reshape(by_token.shape[0], by_token.shape[2])
     wanted_all = lax.all_gather(retrieval, "pool", axis=0, tiled=True)
     reply = jnp.take(by_token, wanted_all, axis=0)
-    fetched = lax.all_to_all(reply[:, :, None, :], "pool", split_axis=0, concat_axis=2, tiled=True)[
-        0
-    ]
+    _define_pieces_all = lambda m: jnp.concatenate(
+        lax.all_to_all(
+            jnp.stack(jnp.split(m, lax.axis_size("pool"), axis=0), axis=0), "pool", 0, 0
+        ),
+        axis=2,
+    )
+    fetched = _define_pieces_all(reply[:, :, None, :])[0]
     count = hidden_rows.shape[0]
     fetch_count = wanted.shape[0]
     group = QH // KVH

time: 441 us -> 519 us (1.18)
  the two profiles are of different devices: /device:TPU:4 before, /device:TPU:2 now
where the time goes in v1:
time: 519 us; the launch traced here: 518 us
  waiting for transfers between devices  214 us (41%)
  local copies, waits for them, and re-layouts  130 us (25%)
  blocking collectives  95.1 us (18%)
  starting transfers between devices  30.7 us (6%)
  matrix products  20.2 us (4%)
  between operations  14.2 us (3%)
  other arithmetic  13.1 us (3%)
    all_gather x1, waiting for transfers between devices, body(): lax.all_gather(kv_weight, 'pool', axis=1, tiled=True)  184 us
    all_gather x1, blocking collectives, body(): wanted_all = lax.all_gather(retrieval, 'pool', axis=0, tiled=True)  95.1 us
    unnamed x134, local copies, waits for them, and re-layouts  80 us
    gather x1, local copies, waits for them, and re-layouts, body(): reply = jnp.take(by_token, wanted_all, axis=0)  33.1 us
    reduce_scatter x1, waiting for transfers between devices, body(): lax.psum_scatter(partial_kv.astype(jnp.bfloat16), 'tp', scatter_dimension...  28.9 us
    all_to_all x1, starting transfers between devices, body(): lax.all_to_all(cache_table, 'pool', split_axis=1, concat_axis=0, tiled=True)  19.5 us
    all_to_all x1, starting transfers between devices, body(): lax.all_to_all(jnp.stack(jnp.split(m, lax.axis_size('pool'), axis=0), axi...  10.9 us
  transfers between devices with their start and end apart: 4, of which 2 were waited for; matrix products, arithmetic and copies ran while one was open for 1% of the time, Pallas kernels for 0%

profile of v1, /device:TPU:2, one launch (start us, length us, event | category | flops | bytes accessed | tf_op | source)
XLA Modules:
  0.0 517.7 jit_solution(1415827210770720806)
XLA Ops:
  7.2 2.2 copy.19
  9.4 19.5 %all-to-all-start = ((bf16[8,128,256]{2,0,1:T(8,128)(2,1)}), bf16[8,128,256]{2,0,1:T(8,128)(2,1)S(1)}, u32[]{:S(2)}, u32[]{:S(2)}) async-start(bf16[8,128,256]{2,0,1:T(8,128)(2,1)} %copy.19), calls=%async_computation.1 | async-start | bytes 1048576 | tf_op jit(solution)/shard_map/all_to_all | solution.py:29
  28.9 95.1 %all-gather = s32[128,1,64]{2,1,0:T(1,128)S(1)} all-gather(s32[1,1,64]{2,1,0:T(1,128)} %bitcast.584), channel_id=1, replica_groups=mesh['pool'=128,'tp'=4] {'pool'}, dimensions={0}, use_global_device_ids=true | all-gather | bytes 33024 | tf_op jit(solution)/shard_map/all_gather | solution.py:31
  124.1 33.1 %gather_fusion = bf16[8192,256]{1,0:T(8,128)(2,1)} fusion(bf16[1024,256]{1,0:T(8,128)(2,1)S(1)} %bitcast.577, s32[8192]{0:T(1024)S(1)} %broadcast_clamp_fusion), kind=kCustom, calls=%fused_computation | custom fusion | bytes 8421376 | tf_op jit(solution)/shard_map/jit(_take)/gather | solution.py:32
  157.2 4.4 broadcast_select_fusion
  168.9 0.6 constant_dynamic-update-slice_fusion.115
  240.1 10.9 %all-to-all-start.1 = ((bf16[128,1,64,1,256]{4,2,3,1,0:T(8,128)(2,1)}), bf16[128,1,64,1,256]{4,2,3,1,0:T(8,128)(2,1)}, u32[]{:S(2)}, u32[]{:S(2)}) async-start(bf16[128,1,64,1,256]{4,2,3,1,0:T(8,128)(2,1)} %constant_dynamic-update-slice_fusion), calls=%async_computation.2 | async-start | bytes 8388608 | tf_op jit(solution)/shard_map/all_to_all | solution.py:34
  251.1 0.7 all-gather.3.cloned.1.call-update
  252.0 184.2 %all-gather.3.cloned.1.call-done = bf16[2048,1024]{0,1:T(8,128)(2,1)} async-done(((bf16[2048,8]{0,1:T(8,128)(2,1)}), bf16[2048,1024]{0,1:T(8,128)(2,1)}) %all-gather.3.cloned.1.call-update) | async-done | bytes 4194320 | tf_op jit(solution)/shard_map/all_gather | solution.py:23
  436.1 4.4 convolution_convert_fusion
  440.8 28.9 %reduce-scatter.2.cloned.1.call-done = bf16[128,256]{1,0:T(8,128)(2,1)} async-done(((bf16[128,1024]{1,0:T(8,128)(2,1)}), bf16[128,256]{1,0:T(8,128)(2,1)}) %reduce-scatter.2.cloned.1.call-update) | async-done | bytes 65552 | tf_op jit(solution)/shard_map/reduce_scatter | solution.py:26
  469.7 1.0 select_reduce_fusion
  470.8 1.0 fusion.12
  471.9 6.5 %copy.20 = bf16[1,64,128,1,256]{4,2,1,3,0:T(8,128)(2,1)} copy(bf16[1,64,128,1,256]{4,1,3,0,2:T(8,128)(2,1)} %bitcast.136) | data formatting | bytes 8388608 | tf_op jit(solution)/shard_map/reshape | solution.py:33
  478.4 31.4 %while.15 = (s32[]{:T(128)}, f32[1024]{0:T(1024)S(1)}, f32[1024]{0:T(1024)S(1)}, f32[1024,128]{1,0:T(8,128)S(1)}, s32[8,2,8]{2,0,1:T(8,128)S(1)}, /*index=5*/bf1...) while((s32[]{:T(128)}, f32[1024]{0:T(1024)S(1)}, ...), condition=%wide.region_7.8_spmd.clone, body=%wide.region_3.7_spmd.clone.sunk | while | flops 545550336 | bytes 15561029 | solution.py:83
  478.5 1.1 dynamic-slice_bitcast_fusion.2
  479.6 0.7 fusion.38
  480.3 0.9 fusion.39
  481.3 1.0 convolution_add_fusion.2
  482.4 1.1 dynamic-slice_bitcast_fusion.2
  483.5 0.7 fusion.38
  484.3 0.9 fusion.39
  485.2 1.0 convolution_add_fusion.2
  486.4 1.1 dynamic-slice_bitcast_fusion.2
  487.5 0.7 fusion.38
  488.2 0.9 fusion.39
  489.2 1.0 convolution_add_fusion.2
  490.3 1.1 dynamic-slice_bitcast_fusion.2
  491.4 0.7 fusion.38
  492.1 0.9 fusion.39
  493.1 1.0 convolution_add_fusion.2
  494.2 1.1 dynamic-slice_bitcast_fusion.2
  495.3 0.7 fusion.38
  496.1 0.9 fusion.39
  497.0 1.0 convolution_add_fusion.2
  498.2 1.1 dynamic-slice_bitcast_fusion.2
  499.2 0.7 fusion.38
  500.0 0.9 fusion.39
  501.0 1.0 convolution_add_fusion.2
  502.1 1.1 dynamic-slice_bitcast_fusion.2
  503.2 0.7 fusion.38
  503.9 0.9 fusion.39
  504.9 1.0 convolution_add_fusion.2
  506.0 1.1 dynamic-slice_bitcast_fusion.2
  507.1 0.7 fusion.38
  507.9 0.9 fusion.39
  508.8 1.0 convolution_add_fusion.2
  510.0 0.8 convert_element_type.18
  (204 shorter events, 79.7 us)
Async XLA Ops:
  7.2 429.0 %copy-start = (bf16[128,2048]{1,0:T(8,128)(2,1)S(1)}, bf16[128,2048]{1,0:T(8,128)(2,1)}, u32[]{:S(2)}) copy-start(bf16[128,2048]{1,0:T(8,128)(2,1)} %param.8) | copy-start | bytes 1572868
  9.4 114.7 %all-to-all-start = ((bf16[8,128,256]{2,0,1:T(8,128)(2,1)}), bf16[8,128,256]{2,0,1:T(8,128)(2,1)S(1)}, u32[]{:S(2)}, u32[]{:S(2)}) async-start(bf16[8,128,256]{2,0,1:T(8,128)(2,1)} %copy.19), calls=%async_computation.1 | async-start | bytes 1048576 | tf_op jit(solution)/shard_map/all_to_all | solution.py:29
  240.1 231.8 %all-to-all-start.1 = ((bf16[128,1,64,1,256]{4,2,3,1,0:T(8,128)(2,1)}), bf16[128,1,64,1,256]{4,2,3,1,0:T(8,128)(2,1)}, u32[]{:S(2)}, u32[]{:S(2)}) async-start(bf16[128,1,64,1,256]{4,2,3,1,0:T(8,128)(2,1)} %constant_dynamic-update-slice_fusion), calls=%async_computation.2 | async-start | bytes 8388608 | tf_op jit(solution)/shard_map/all_to_all | solution.py:34
  251.0 189.6 %copy-start.1 = (bf16[128,1024]{1,0:T(8,128)(2,1)S(1)}, bf16[128,1024]{1,0:T(8,128)(2,1)}, u32[]{:S(2)}) copy-start(bf16[128,1024]{1,0:T(8,128)(2,1)} %param.10) | copy-start | bytes 786436
  251.0 189.7 %copy-start.2 = (s32[1,2,64]{2,1,0:T(2,128)S(1)}, s32[1,2,64]{2,1,0:T(2,128)}, u32[]{:S(2)}) copy-start(s32[1,2,64]{2,1,0:T(2,128)} %param.13) | copy-start | bytes 1540
  251.0 185.1 %all-gather.3.cloned.1.call-start = ((), (), s32[]{:S(2)}) async-start(), calls=%async_computation.3 | async-start | bytes 4227072 | tf_op jit(solution)/shard_map/all_gather | solution.py:23
  251.8 217.9 %reduce-scatter.2.cloned.1.call-start = ((), (), s32[]{:S(2)}) async-start(), calls=%async_computation.4 | async-start | bytes 327680 | tf_op jit(solution)/shard_map/reduce_scatter | solution.py:26
Sparse Core Ops, SparseCore 0:
  255.0 181.1 all-gather.2
  440.7 28.9 reduce-scatter.1
